TPU v7x, 512 devices: a whole 4x4x16 slice. The times are simulated.
512 devices in a mesh: panel: 2 (over x_lo), lat: 8 (over y, core), lon: 32 (over z, x_hi).
Axes of the slice: x: 4 (x_hi: 2, x_lo: 2; x = x_hi * 2 + x_lo), y: 4, z: 16, core: 2. Of those that a mesh axis runs over, the one named last changes fastest.
Arguments:
- fields: float32 [2, 6, 4, 1024, 4096], P('panel', None, None, 'lat', 'lon'), may hold values from -6 to 6
- viscosity: float32 [2, 4, 1024, 4096], P('panel', None, 'lat', 'lon'), may hold values from 0.01 to 0.1
- partner: int32 [2, 8, 1024, 1], P('panel', 'lat', 'lon'), may hold values from 0 to 31; in each aligned block of 32 rows (0 to 31, 32 to 63, ..., all dimensions but the last counted through in order) at most 2 rows name the same one
- src_row: int32 [2, 8, 65536], P('panel', 'lat', 'lon'), may hold values from 0 to 126
- src_col: int32 [2, 8, 65536], P('panel', 'lat', 'lon'), may hold values from 0 to 126
- weight_id: int32 [2, 8, 65536], P('panel', 'lat', 'lon'), may hold values from 0 to 63
- border_angle: float32 [2, 8, 65536], P('panel', 'lat', 'lon'), may hold values from -3.140625 to 3.140625
- dest_cell: int32 [2, 8, 65536], P('panel', 'lat', 'lon'), may hold values from 0 to 16383, as said below
Outputs:
- new_fields: float32 [2, 6, 4, 1024, 4096], P('panel', None, None, 'lat', 'lon')
- pressure: float32 [2, 4, 1024, 4096], P('panel', None, 'lat', 'lon')
Inputs may be any that keep to these rules, and one draw needn't show every extreme that they name: `partner`: A border block's sources lie on the device of the other panel with the same lat index and this lon index; among the 32 blocks of one device no lon index is named by more than 2 blocks. `dest_cell`: the 2048 border cells of one device are distinct cells of its block.
All inputs are finite; a program needn't handle non-finite values.
Results may differ from a plain program's by a relative error of at most 0.0002.
Values sent between devices are 32-bit elements; how exact they have to be, the bound alone decides.
No kernel may reach another device: no remote copies, remote signals or barrier semaphores. Data moves between devices by JAX's collectives and lax.ppermute only.
A program may use at most 128 MiB of HBM per device.

v0:
```python
import math
import jax
import jax.numpy as jnp
from jax import lax
from jax.sharding import PartitionSpec as P

CAP = 2
WQ = 8
BUOYANCY = 0.5


def partner_2(block, axis, apart):
    count = lax.axis_size(axis)
    route = []
    for low in range(count):
        high = low | 1 << apart
        if high != low and high < count:
            route += [(low, high), (high, low)]
    return lax.ppermute(block, axis, route)


def padded_2(shard, sides, width):
    for axis, dim in sides:
        size, length = (lax.axis_size(axis), shard.shape[dim])
        up = [(i, (i + 1) % size) for i in range(size - 1)]
        down = [(j, i) for i, j in up]
        last = lax.slice_in_dim(shard, length - width, length, axis=dim)
        leading = lax.slice_in_dim(shard, 0, width, axis=dim)
        before = lax.ppermute(last, axis, up)
        after = lax.ppermute(leading, axis, down)
        shard = jnp.concatenate([before, shard, after], axis=dim)
    return shard


def metric(row_index, total_rows):
    colatitude = (
        math.pi / 4.0 + (row_index.astype(jnp.float32) + 0.5) * (math.pi / 2.0) / total_rows
    )
    inv_sine = 1.0 / jnp.sin(colatitude)
    return (inv_sine, inv_sine * inv_sine)


def lap_shrink(field, row_gain):
    centre = field[..., 1:-1, 1:-1]
    padded = jnp.pad(centre, [(0, 0)] * (centre.ndim - 3) + [(1, 1), (0, 0), (0, 0)])
    lat_term = field[..., 2:, 1:-1] + field[..., :-2, 1:-1] - 2.0 * centre
    lon_term = field[..., 1:-1, 2:] + field[..., 1:-1, :-2] - 2.0 * centre
    radial = padded[..., 2:, :, :] + padded[..., :-2, :, :] - 2.0 * centre
    return lat_term + row_gain[:, None] * lon_term + radial


def diverge(velocity, inv_sine):
    radial_pad = jnp.pad(velocity[0, :, 1:-1, 1:-1], ((1, 1), (0, 0), (0, 0)))
    lat_part = velocity[1, :, 2:, 1:-1] - velocity[1, :, :-2, 1:-1]
    lon_part = velocity[2, :, 1:-1, 2:] - velocity[2, :, 1:-1, :-2]
    rad_part = radial_pad[2:] - radial_pad[:-2]
    return 0.5 * (lat_part + inv_sine[:, None] * lon_part + rad_part)


def gradient(pressure, inv_sine):
    radial_pad = jnp.pad(pressure[:, 1:-1, 1:-1], ((1, 1), (0, 0), (0, 0)))
    grad_rad = 0.5 * (radial_pad[2:] - radial_pad[:-2])
    grad_lat = 0.5 * (pressure[:, 2:, 1:-1] - pressure[:, :-2, 1:-1])
    grad_lon = 0.5 * inv_sine[:, None] * (pressure[:, 1:-1, 2:] - pressure[:, 1:-1, :-2])
    return (grad_rad, grad_lat, grad_lon)


def cosine_table(length):
    mode_ids = jnp.arange(length, dtype=jnp.float32)
    cell_mid = jnp.arange(length, dtype=jnp.float32) + 0.5
    row_norm = jnp.sqrt(jnp.where(mode_ids > 0, 2.0, 1.0) / length)
    cos_table = row_norm[:, None] * jnp.cos(
        math.pi * mode_ids[:, None] * cell_mid[None, :] / length
    )
    eigenvalue = 4.0 * jnp.sin(math.pi * mode_ids / (2.0 * length)) ** 2
    return (cos_table, eigenvalue)


def coarse_divisor(levels, n_lat, n_lon):
    eig_rad = cosine_table(levels)[1]
    eig_lat = cosine_table(n_lat)[1]
    eig_lon = cosine_table(n_lon)[1]
    return (
        eig_rad[:, None, None]
        + eig_lat[None, :, None]
        + eig_lon[None, None, :]
        + 1.0 / (n_lat * n_lon)
    )


def coarse_solve(block_sum, n_lat, n_lon):
    highest = lax.Precision.HIGHEST
    tab_rad = cosine_table(block_sum.shape[0])[0]
    tab_lat = cosine_table(n_lat)[0]
    tab_lon = cosine_table(n_lon)[0]
    spectrum = jnp.einsum("kr,rlo->klo", tab_rad, block_sum, precision=highest)
    spectrum = jnp.einsum("kl,rlo->rko", tab_lat, spectrum, precision=highest)
    spectrum = jnp.einsum("ko,rlo->rlk", tab_lon, spectrum, precision=highest)
    spectrum = spectrum / coarse_divisor(block_sum.shape[0], n_lat, n_lon)
    restored = jnp.einsum("kr,klo->rlo", tab_rad, spectrum, precision=highest)
    restored = jnp.einsum("kl,rko->rlo", tab_lat, restored, precision=highest)
    restored = jnp.einsum("ko,rlk->rlo", tab_lon, restored, precision=highest)
    return restored / math.sqrt(n_lat * n_lon)


def fractions(weight_ids):
    frac_lat = ((weight_ids // WQ).astype(jnp.float32) + 0.5) / WQ
    frac_lon = ((weight_ids % WQ).astype(jnp.float32) + 0.5) / WQ
    return (frac_lat, frac_lon)


def bilinear(lower_left, lower_right, upper_left, upper_right, frac_lat, frac_lon):
    return (
        (1.0 - frac_lat) * (1.0 - frac_lon) * lower_left
        + (1.0 - frac_lat) * frac_lon * lower_right
        + frac_lat * (1.0 - frac_lon) * upper_left
        + frac_lat * frac_lon * upper_right
    )


def shards(fields, viscosity, partner, src_row, src_col, weight_id, border_angle, dest_cell):
    n_lat = lax.axis_size("lat")
    n_lon = lax.axis_size("lon")
    lat_pos = lax.axis_index("lat")
    lon_pos = lax.axis_index("lon")
    own_fields = fields[0]
    levels, rows_dev, cols_dev = (own_fields.shape[1], own_fields.shape[2], own_fields.shape[3])
    channels = 6 * levels
    blocks = partner.shape[2]
    block_cells = src_row.shape[2] // blocks
    capacity = CAP
    slot_count = n_lon * capacity
    total_rows = rows_dev * n_lat
    flat_cells = own_fields.reshape(channels, rows_dev * cols_dev)
    target = partner[0, 0, :, 0]
    onehot = (target[:, None] == jnp.arange(n_lon, dtype=jnp.int32)[None, :]).astype(jnp.int32)
    before = jnp.sum(
        (jnp.cumsum(onehot, axis=0, dtype=jnp.int32) - onehot) * onehot, axis=1, dtype=jnp.int32
    )
    slot_of = target * capacity + before
    base_cell = (src_row[0, 0] * cols_dev + src_col[0, 0]).reshape(blocks, block_cells)
    weight_ids = weight_id[0, 0].reshape(blocks, block_cells)
    empty = jnp.zeros((slot_count, block_cells), jnp.int32)
    requests = partner_2(
        empty.at[slot_of].set(base_cell).reshape(n_lon, capacity * block_cells), "panel", 0
    )
    requests = lax.all_to_all(requests, "lon", split_axis=0, concat_axis=0, tiled=True)
    served = jnp.stack(
        tuple(
            (
                jnp.take(flat_cells, requests + offset, axis=1)
                for offset in (0, 1, cols_dev, cols_dev + 1)
            )
        ),
        axis=0,
    )
    served = lax.all_to_all(served, "lon", split_axis=2, concat_axis=2, tiled=True)
    served = partner_2(served, "panel", 0)
    picked = served.reshape(4, channels, slot_count, block_cells)[:, :, slot_of, :]
    frac_lat, frac_lon = fractions(weight_ids)
    values = bilinear(picked[0], picked[1], picked[2], picked[3], frac_lat, frac_lon)
    values = values.reshape(6, levels, blocks * block_cells)
    turn = border_angle[0, 0]
    cos_angle = jnp.cos(turn)
    sin_angle = jnp.sin(turn)
    rotated = jnp.stack(
        [
            values[0],
            cos_angle * values[1] + sin_angle * values[2],
            cos_angle * values[2] - sin_angle * values[1],
            values[3],
            cos_angle * values[4] + sin_angle * values[5],
            cos_angle * values[5] - sin_angle * values[4],
        ],
        axis=0,
    ).reshape(channels, blocks * block_cells)
    filled = flat_cells.at[:, dest_cell[0, 0]].set(rotated).reshape(6, levels, rows_dev, cols_dev)
    diffusivity = viscosity[0]
    inv_own, gain_own = metric(
        lat_pos * rows_dev + jnp.arange(-0, rows_dev + 0, dtype=jnp.int32), total_rows
    )
    widened = padded_2(filled, (("lat", 2), ("lon", 3)), 1)
    stepped = filled + diffusivity[None] * lap_shrink(widened, gain_own)
    stepped = jnp.concatenate([stepped[0:1] + BUOYANCY * filled[3:4], stepped[1:]], axis=0)
    velocity = padded_2(stepped[0:3], (("lat", 2), ("lon", 3)), 1)
    divergence = diverge(velocity, inv_own)
    press_one = -divergence / (4.0 + 2.0 * gain_own)[:, None]
    press_wide = padded_2(press_one, (("lat", 1), ("lon", 2)), 1)
    resid_one = -divergence + lap_shrink(press_wide, gain_own)
    block_sum = jnp.sum(resid_one, axis=(1, 2)) * (1.0 / math.sqrt(rows_dev * cols_dev))
    gathered = lax.all_gather(block_sum[:, None], ("lat", "lon"), axis=1, tiled=True)
    coarse = coarse_solve(gathered.reshape(levels, n_lat, n_lon), n_lat, n_lon)
    start = jnp.zeros((), jnp.int32)
    own_coarse = lax.dynamic_slice(coarse, (start, lat_pos, lon_pos), (levels, 1, 1)).reshape(
        levels
    )
    pressure = press_one + own_coarse[:, None, None]
    press_rim = padded_2(pressure, (("lat", 1), ("lon", 2)), 1)
    grad_rad, grad_lat, grad_lon = gradient(press_rim, inv_own)
    result = jnp.stack(
        [
            stepped[0] - grad_rad,
            stepped[1] - grad_lat,
            stepped[2] - grad_lon,
            stepped[3],
            stepped[4],
            stepped[5],
        ],
        axis=0,
    )
    return (result[None], pressure[None])


def solution(mesh):
    return jax.shard_map(
        shards,
        mesh=mesh,
        in_specs=(
            P("panel", None, None, "lat", "lon"),
            P("panel", None, "lat", "lon"),
            P("panel", "lat", "lon", None),
            P("panel", "lat", "lon"),
            P("panel", "lat", "lon"),
            P("panel", "lat", "lon"),
            P("panel", "lat", "lon"),
            P("panel", "lat", "lon"),
        ),
        out_specs=(P("panel", None, None, "lat", "lon"), P("panel", None, "lat", "lon")),
        check_vma=False,
    )
```

profile of v0, /device:TPU:32, one launch (start us, length us, event | category | flops | bytes accessed | tf_op | source)
XLA Modules:
  0.0 1006.0 jit_solution(13711686433813685990)
XLA Ops:
  1.4 0.8 select_reduce_fusion
  4.5 3.4 collective-permute-start
  7.9 2.3 collective-permute-done
  10.2 17.8 %all-to-all-start = ((s32[32,1,128]{2,1,0:T(1,128)}), s32[32,1,128]{2,1,0:T(1,128)S(1)}, u32[]{:S(2)}, u32[]{:S(2)}) async-start(s32[32,1,128]{2,1,0:T(1,128)} %bitcast.6), calls=%async_computation | async-start | bytes 32768 | tf_op jit(solution)/shard_map/all_to_all | solution.py:147
  28.0 2.3 copy.132
  30.4 4.7 copy.95
  35.0 6.4 all-to-all-done
  41.5 14.1 %gather_fusion.1 = f32[4096,24]{1,0:T(8,128)S(1)} fusion(f32[24,16384]{0,1:T(8,128)} %copy.95, s32[4096]{0:T(1024)S(1)} %get-tuple-element.38), kind=kCustom, calls=%fused_computation.clone | custom fusion | bytes 802816 | tf_op jit(solution)/shard_map/jit(_take)/gather | solution.py:151
  56.2 14.1 %gather_fusion.2 = f32[4096,24]{1,0:T(8,128)S(1)} fusion(f32[24,16384]{0,1:T(8,128)} %copy.95, s32[4096]{0:T(1024)S(1)} %get-tuple-element.39), kind=kCustom, calls=%fused_computation.1.clone | custom fusion | bytes 802816 | tf_op jit(solution)/shard_map/jit(_take)/gather | solution.py:151
  71.0 14.1 %gather_fusion.3 = f32[4096,24]{1,0:T(8,128)S(1)} fusion(f32[24,16384]{0,1:T(8,128)} %copy.95, s32[4096]{0:T(1024)S(1)} %get-tuple-element.40), kind=kCustom, calls=%fused_computation.2.clone | custom fusion | bytes 802816 | tf_op jit(solution)/shard_map/jit(_take)/gather | solution.py:151
  85.7 14.1 %gather_fusion.4 = f32[4096,24]{1,0:T(8,128)S(1)} fusion(f32[24,16384]{0,1:T(8,128)} %copy.95, s32[4096]{0:T(1024)S(1)} %get-tuple-element.41), kind=kCustom, calls=%fused_computation.3.clone | custom fusion | bytes 802816 | tf_op jit(solution)/shard_map/jit(_take)/gather | solution.py:151
  99.8 1.3 copy.83
  101.3 0.9 copy-done
  102.2 1.2 pad_maximum_fusion.9
  103.5 8.3 all-to-all-start.1
  111.9 73.8 %all-to-all-done.1 = f32[4,24,32,128]{3,1,0,2:T(8,128)S(1)} async-done(((f32[4,24,32,128]{3,1,0,2:T(8,128)}), f32[4,24,32,128]{3,1,0,2:T(8,128)S(1)}, u32[]{:S(2)}, u32[]{:S(2)}) %all-to-all-start.1) | async-done | bytes 1572896 | tf_op jit(solution)/shard_map/all_to_all | solution.py:157
  185.8 2.5 collective-permute-start.1
  190.0 26.9 %collective-permute-done.1 = f32[4,24,32,128]{3,1,0,2:T(8,128)S(1)} collective-permute-done((f32[4,24,32,128]{3,1,0,2:T(8,128)S(1)}, f32[4,24,32,128]{3,1,0,2:T(8,128)S(1)}, u32[]{:S(2)}, u32[]{:S(2)}) %collective-permute-start.1) | collective-permute-done | bytes 1572896 | tf_op jit(solution)/shard_map/ppermute | solution.py:19
  216.9 2.1 copy.84
  219.0 2.4 reshape.638
  221.4 3.5 copy.85
  224.9 2.5 gather_fusion
  228.9 12.2 %scatter_fusion = f32[24,16384]{0,1:T(8,128)} fusion(f32[24,16384]{0,1:T(8,128)} %copy.95, s32[2048]{0:T(1024)S(1)} %bitcast.183, f32[2048,24]{1,0:T(8,128)S(1)} %copy.96), kind=kCustom, calls=%fused_computation.6 | custom fusion | bytes 598016 | tf_op jit(solution)/shard_map/scatter | solution.py:177
  241.1 5.1 copy.97
  246.5 1.3 collective-permute-start.2
  247.8 3.0 collective-permute-start.3
  250.9 0.8 collective-permute-done.3
  251.8 2.3 fusion.116
  254.1 2.3 copy.100
  256.4 7.6 collective-permute-start.5
  264.1 2.3 copy.98
  266.4 4.8 collective-permute-start.4
  271.2 6.6 slice_multiply_fusion
  277.8 5.2 copy.102
  283.0 1.8 copy.101
  284.8 1.8 copy.99
  286.6 3.5 fusion.4
  290.3 1.3 collective-permute-start.6
  291.6 3.4 collective-permute-start.7
  295.9 1.4 fusion.118
  297.4 1.6 copy.103
  299.0 5.1 collective-permute-start.8
  304.1 1.6 copy.105
  305.7 2.2 collective-permute-start.9
  308.0 1.3 copy.104
  309.2 4.5 collective-permute-done.9
  313.7 1.2 copy.106
  315.0 1.4 broadcast_divide_fusion
  316.4 1.3 collective-permute-start.10
  317.7 3.9 collective-permute-start.11
  321.6 0.8 collective-permute-done.11
  322.4 0.8 fusion.121
  323.2 2.4 collective-permute-start.12
  325.6 4.9 collective-permute-start.13
  330.5 9.0 collective-permute-done.12
  340.0 638.4 %all-gather = f32[256,1,4]{2,1,0:T(1,128)S(1)} all-gather(f32[1,1,4]{2,1,0:T(1,128)S(1)} %multiply_bitcast_fusion), channel_id=1, replica_groups=mesh['panel'=2,'lat'=8,'lon'=32] {'lat','lon'}, dimensions={0}, use_global_device_ids=true | all-gather | bytes 4112 | tf_op jit(solution)/shard_map/all_gather | solution.py:191
  978.3 0.7 fusion.80
  980.8 1.3 collective-permute-start.14
  982.1 3.0 collective-permute-start.15
  986.1 2.6 collective-permute-start.16
  988.8 4.7 collective-permute-start.17
  993.5 0.8 fusion.128
  994.3 10.1 %collective-permute-done.16 = f32[4,130,1]{2,1,0:T(8,128)S(1)} collective-permute-done((f32[4,130,1]{2,1,0:T(8,128)S(1)}, f32[4,130,1]{2,1,0:T(8,128)S(1)}, u32[]{:S(2)}, u32[]{:S(2)}) %collective-permute-start.16) | collective-permute-done | bytes 2112 | tf_op jit(solution)/shard_map/ppermute | solution.py:30
  1004.8 1.3 maximum_bitcast_fusion
  (97 shorter events, 13.1 us)
Async XLA Ops:
  4.5 5.7 collective-permute-start
  10.2 31.2 %all-to-all-start = ((s32[32,1,128]{2,1,0:T(1,128)}), s32[32,1,128]{2,1,0:T(1,128)S(1)}, u32[]{:S(2)}, u32[]{:S(2)}) async-start(s32[32,1,128]{2,1,0:T(1,128)} %bitcast.6), calls=%async_computation | async-start | bytes 32768 | tf_op jit(solution)/shard_map/all_to_all | solution.py:147
  101.2 1.0 copy-start
  103.5 85.3 %copy-start.2 = (s32[1,1,2048]{2,1,0:T(1,128)S(1)}, s32[1,1,2048]{2,1,0:T(1,128)}, u32[]{:S(2)}) copy-start(s32[1,1,2048]{2,1,0:T(1,128)} %param.15) | copy-start | bytes 24580
  103.5 86.2 %copy-start.3 = (s32[1,1,2048]{2,1,0:T(1,128)S(1)}, s32[1,1,2048]{2,1,0:T(1,128)}, u32[]{:S(2)}) copy-start(s32[1,1,2048]{2,1,0:T(1,128)} %param.17) | copy-start | bytes 24580
  103.5 86.3 %copy-start.1 = (f32[1,1,2048]{2,1,0:T(1,128)S(1)}, f32[1,1,2048]{2,1,0:T(1,128)}, u32[]{:S(2)}) copy-start(f32[1,1,2048]{2,1,0:T(1,128)} %param.16) | copy-start | bytes 24580
  103.5 82.3 %all-to-all-start.1 = ((f32[4,24,32,128]{3,1,0,2:T(8,128)}), f32[4,24,32,128]{3,1,0,2:T(8,128)S(1)}, u32[]{:S(2)}, u32[]{:S(2)}) async-start(f32[4,24,32,128]{3,1,0,2:T(8,128)} %pad_maximum_fusion.9), calls=%async_computation.1 | async-start | bytes 3145728 | tf_op jit(solution)/shard_map/all_to_all | solution.py:157
  185.8 31.2 %collective-permute-start.1 = (f32[4,24,32,128]{3,1,0,2:T(8,128)S(1)}, f32[4,24,32,128]{3,1,0,2:T(8,128)S(1)}, u32[]{:S(2)}, u32[]{:S(2)}) collective-permute-start(f32[4,24,32,128]{3,1,0,2:T(8,128)S(1)} %all-to-all-done.1), channel_id=1, source_target_pairs={{0,256},{256,0},{1,257},{257,1},{2,258},{258,2},{3,259},{259,3},{4... | collective-permute-start | bytes 4718600 | tf_op jit(solution)/shard_map/ppermute | solution.py:19
  246.5 4.4 collective-permute-start.2
  247.8 3.9 collective-permute-start.3
  256.4 26.6 %collective-permute-start.5 = (f32[6,4,130,1]{2,1,3,0:T(4,128)S(1)}, f32[6,4,130,1]{2,1,3,0:T(4,128)S(1)}, u32[]{:S(2)}, u32[]{:S(2)}) collective-permute-start(f32[6,4,130,1]{2,1,3,0:T(4,128)S(1)} %copy.100), channel_id=1, source_target_pairs={{0,1},{1,2},{2,3},{3,4},{4,5},{5,6},{6,7},{7,8},{8,9},{9,10},{10,1... | collective-permute-start | bytes 37448 | tf_op jit(solution)/shard_map/ppermute | solution.py:29
  266.4 18.4 %collective-permute-start.4 = (f32[6,4,130,1]{2,1,3,0:T(4,128)S(1)}, f32[6,4,130,1]{2,1,3,0:T(4,128)S(1)}, u32[]{:S(2)}, u32[]{:S(2)}) collective-permute-start(f32[6,4,130,1]{2,1,3,0:T(4,128)S(1)} %copy.98), channel_id=1, source_target_pairs={{1,0},{2,1},{3,2},{4,3},{5,4},{6,5},{7,6},{8,7},{9,8},{10,9},{11,1... | collective-permute-start | bytes 37448 | tf_op jit(solution)/shard_map/ppermute | solution.py:30
  290.3 4.8 collective-permute-start.6
  291.6 4.3 collective-permute-start.7
  299.0 9.0 collective-permute-start.8
  305.7 8.0 collective-permute-start.9
  316.4 5.2 collective-permute-start.10
  317.7 4.7 collective-permute-start.11
  323.2 16.4 %collective-permute-start.12 = (f32[4,130,1]{2,1,0:T(8,128)}, f32[4,130,1]{2,1,0:T(8,128)S(1)}, u32[]{:S(2)}, u32[]{:S(2)}) collective-permute-start(f32[4,130,1]{2,1,0:T(8,128)} %get-tuple-element.23), channel_id=1, source_target_pairs={{1,0},{2,1},{3,2},{4,3},{5,4},{6,5},{7,6},{8,7},{9,8},{10,9},{11,1... | collective-permute-start | bytes 6248 | tf_op jit(solution)/shard_map/ppermute | solution.py:30
  325.6 14.0 %collective-permute-start.13 = (f32[4,130,1]{2,1,0:T(8,128)S(1)}, f32[4,130,1]{2,1,0:T(8,128)S(1)}, u32[]{:S(2)}, u32[]{:S(2)}) collective-permute-start(f32[4,130,1]{2,1,0:T(8,128)S(1)} %get-tuple-element.24), channel_id=1, source_target_pairs={{0,1},{1,2},{2,3},{3,4},{4,5},{5,6},{6,7},{7,8},{8,9},{9,10},{10,1... | collective-permute-start | bytes 6248 | tf_op jit(solution)/shard_map/ppermute | solution.py:29
  980.8 4.5 collective-permute-start.14
  982.1 3.8 collective-permute-start.15
  986.1 18.3 %collective-permute-start.16 = (f32[4,130,1]{2,1,0:T(8,128)S(1)}, f32[4,130,1]{2,1,0:T(8,128)S(1)}, u32[]{:S(2)}, u32[]{:S(2)}) collective-permute-start(f32[4,130,1]{2,1,0:T(8,128)S(1)} %get-tuple-element.21), channel_id=1, source_target_pairs={{1,0},{2,1},{3,2},{4,3},{5,4},{6,5},{7,6},{8,7},{9,8},{10,9},{11,1... | collective-permute-start | bytes 6248 | tf_op jit(solution)/shard_map/ppermute | solution.py:30
  988.8 15.6 %collective-permute-start.17 = (f32[4,130,1]{2,1,0:T(8,128)S(1)}, f32[4,130,1]{2,1,0:T(8,128)S(1)}, u32[]{:S(2)}, u32[]{:S(2)}) collective-permute-start(f32[4,130,1]{2,1,0:T(8,128)S(1)} %get-tuple-element.22), channel_id=1, source_target_pairs={{0,1},{1,2},{2,3},{3,4},{4,5},{5,6},{6,7},{7,8},{8,9},{9,10},{10,1... | collective-permute-start | bytes 6248 | tf_op jit(solution)/shard_map/ppermute | solution.py:29
where the time goes:
time: 1010 us
  blocking collectives  638 us (63%)
  waiting for transfers between devices  136 us (13%)
  local copies, waits for them, and re-layouts  122 us (12%)
  starting transfers between devices  85 us (8%)
  other arithmetic  20.7 us (2%)
    all_gather x1, blocking collectives, shards(): lax.all_gather(block_sum[:, None], ('lat', 'lon'), axis=1, tiled=True)  638 us
    all_to_all x1, waiting for transfers between devices, shards(): lax.all_to_all(served, 'lon', split_axis=2, concat_axis=2, tiled=True)  73.8 us
    gather x8, local copies, waits for them, and re-layouts, shards(): jnp.take(flat_cells, requests + offset, axis=1)  59.6 us
    ppermute x8, starting transfers between devices, padded_2(): before = lax.ppermute(last, axis, up)  32.9 us
    ppermute x2, waiting for transfers between devices, partner_2(): return lax.ppermute(block, axis, route)  29.2 us
  transfers between devices with their start and end apart: 20, of which 11 were waited for; matrix products, arithmetic and copies ran while one was open for 3% of the time, Pallas kernels for 0%

commit v1 on v0

--- a/solution.py
+++ b/solution.py
@@ -188,7 +188,9 @@
     press_wide = padded_2(press_one, (("lat", 1), ("lon", 2)), 1)
     resid_one = -divergence + lap_shrink(press_wide, gain_own)
     block_sum = jnp.sum(resid_one, axis=(1, 2)) * (1.0 / math.sqrt(rows_dev * cols_dev))
-    gathered = lax.all_gather(block_sum[:, None], ("lat", "lon"), axis=1, tiled=True)
+    block_2 = block_sum[:, None]
+    repeated = jnp.stack([block_2] * lax.axis_size(("lat", "lon")))
+    gathered = jnp.concatenate(lax.all_to_all(repeated, ("lat", "lon"), 0, 0), axis=1)
     coarse = coarse_solve(gathered.reshape(levels, n_lat, n_lon), n_lat, n_lon)
     start = jnp.zeros((), jnp.int32)
     own_coarse = lax.dynamic_slice(coarse, (start, lat_pos, lon_pos), (levels, 1, 1)).reshape(

time: 1010 us -> 406 us (0.40)
  blocking collectives: 638 us -> 0 us
  starting transfers between devices: 85 us -> 104 us
  waiting for transfers between devices: 136 us -> 153 us
    all_gather x1 -> x0, blocking collectives: 638 us -> none  [shards(): lax.all_gather(block_sum[:, None], ('lat', 'lon'), axis=1, tiled=True)]
    all_to_all x0 -> x1, starting transfers between devices: none -> 19.3 us  [shards(): lax.all_to_all(repeated, ('lat', 'lon'), 0, 0)]
    all_to_all x0 -> x1, waiting for transfers between devices: none -> 19.2 us  [shards(): lax.all_to_all(repeated, ('lat', 'lon'), 0, 0)]
  transfers between devices with their start and end apart: 20 -> 21, of which waited for: 11 -> 13; matrix products, arithmetic and copies ran while one was open for 3% -> 7% of each run, Pallas kernels for 0% -> 0%
where the time goes in v1:
time: 406 us; the launch traced here: 404 us
  waiting for transfers between devices  153 us (38%)
  local copies, waits for them, and re-layouts  122 us (30%)
  starting transfers between devices  104 us (26%)
  other arithmetic  20.8 us (5%)
    all_to_all x1, waiting for transfers between devices, shards(): lax.all_to_all(served, 'lon', split_axis=2, concat_axis=2, tiled=True)  73.9 us
    gather x8, local copies, waits for them, and re-layouts, shards(): jnp.take(flat_cells, requests + offset, axis=1)  59.6 us
    ppermute x8, starting transfers between devices, padded_2(): before = lax.ppermute(last, axis, up)  31.9 us
    ppermute x2, waiting for transfers between devices, partner_2(): return lax.ppermute(block, axis, route)  29.2 us
    ppermute x8, starting transfers between devices, padded_2(): after = lax.ppermute(leading, axis, down)  21.2 us
    all_to_all x1, starting transfers between devices, shards(): lax.all_to_all(repeated, ('lat', 'lon'), 0, 0)  19.3 us
    all_to_all x1, waiting for transfers between devices, shards(): lax.all_to_all(repeated, ('lat', 'lon'), 0, 0)  19.2 us
    all_to_all x1, starting transfers between devices, shards(): lax.all_to_all(requests, 'lon', split_axis=0, concat_axis=0, tiled=True)  17.8 us
  transfers between devices with their start and end apart: 21, of which 13 were waited for; matrix products, arithmetic and copies ran while one was open for 7% of the time, Pallas kernels for 0%

profile of v1, /device:TPU:32, one launch (start us, length us, event | category | flops | bytes accessed | tf_op | source)
XLA Modules:
  0.0 404.2 jit_solution(4699220876035040230)
XLA Ops:
  1.4 0.8 select_reduce_fusion
  4.5 3.4 collective-permute-start
  7.9 2.3 collective-permute-done
  10.2 17.8 %all-to-all-start = ((s32[32,1,128]{2,1,0:T(1,128)}), s32[32,1,128]{2,1,0:T(1,128)S(1)}, u32[]{:S(2)}, u32[]{:S(2)}) async-start(s32[32,1,128]{2,1,0:T(1,128)} %bitcast.6), calls=%async_computation | async-start | bytes 32768 | tf_op jit(solution)/shard_map/all_to_all | solution.py:147
  28.0 2.3 copy.132
  30.4 4.7 %copy.95 = f32[24,16384]{0,1:T(8,128)} copy(f32[24,16384]{1,0:T(8,128)S(1)} %bitcast.158) | data formatting | bytes 3145728 | tf_op jit(solution)/shard_map/reshape;squeeze | solution.py:134
  35.1 6.4 %all-to-all-done = s32[32,1,128]{2,1,0:T(1,128)S(1)} async-done(((s32[32,1,128]{2,1,0:T(1,128)}), s32[32,1,128]{2,1,0:T(1,128)S(1)}, u32[]{:S(2)}, u32[]{:S(2)}) %all-to-all-start) | async-done | bytes 16416 | tf_op jit(solution)/shard_map/all_to_all | solution.py:147
  41.5 14.1 %gather_fusion.1 = f32[4096,24]{1,0:T(8,128)S(1)} fusion(f32[24,16384]{0,1:T(8,128)} %copy.95, s32[4096]{0:T(1024)S(1)} %get-tuple-element.38), kind=kCustom, calls=%fused_computation.clone | custom fusion | bytes 802816 | tf_op jit(solution)/shard_map/jit(_take)/gather | solution.py:151
  56.2 14.1 %gather_fusion.2 = f32[4096,24]{1,0:T(8,128)S(1)} fusion(f32[24,16384]{0,1:T(8,128)} %copy.95, s32[4096]{0:T(1024)S(1)} %get-tuple-element.39), kind=kCustom, calls=%fused_computation.1.clone | custom fusion | bytes 802816 | tf_op jit(solution)/shard_map/jit(_take)/gather | solution.py:151
  70.9 14.1 %gather_fusion.3 = f32[4096,24]{1,0:T(8,128)S(1)} fusion(f32[24,16384]{0,1:T(8,128)} %copy.95, s32[4096]{0:T(1024)S(1)} %get-tuple-element.40), kind=kCustom, calls=%fused_computation.2.clone | custom fusion | bytes 802816 | tf_op jit(solution)/shard_map/jit(_take)/gather | solution.py:151
  85.7 14.1 %gather_fusion.4 = f32[4096,24]{1,0:T(8,128)S(1)} fusion(f32[24,16384]{0,1:T(8,128)} %copy.95, s32[4096]{0:T(1024)S(1)} %get-tuple-element.41), kind=kCustom, calls=%fused_computation.3.clone | custom fusion | bytes 802816 | tf_op jit(solution)/shard_map/jit(_take)/gather | solution.py:151
  99.8 1.3 copy.83
  101.2 0.9 copy-done
  102.2 1.2 pad_maximum_fusion.9
  103.5 8.3 %all-to-all-start.1 = ((f32[4,24,32,128]{3,1,0,2:T(8,128)}), f32[4,24,32,128]{3,1,0,2:T(8,128)S(1)}, u32[]{:S(2)}, u32[]{:S(2)}) async-start(f32[4,24,32,128]{3,1,0,2:T(8,128)} %pad_maximum_fusion.9), calls=%async_computation.1 | async-start | bytes 3145728 | tf_op jit(solution)/shard_map/all_to_all | solution.py:157
  111.9 73.9 %all-to-all-done.1 = f32[4,24,32,128]{3,1,0,2:T(8,128)S(1)} async-done(((f32[4,24,32,128]{3,1,0,2:T(8,128)}), f32[4,24,32,128]{3,1,0,2:T(8,128)S(1)}, u32[]{:S(2)}, u32[]{:S(2)}) %all-to-all-start.1) | async-done | bytes 1572896 | tf_op jit(solution)/shard_map/all_to_all | solution.py:157
  185.8 2.5 collective-permute-start.1
  190.0 26.9 %collective-permute-done.1 = f32[4,24,32,128]{3,1,0,2:T(8,128)S(1)} collective-permute-done((f32[4,24,32,128]{3,1,0,2:T(8,128)S(1)}, f32[4,24,32,128]{3,1,0,2:T(8,128)S(1)}, u32[]{:S(2)}, u32[]{:S(2)}) %collective-permute-start.1) | collective-permute-done | bytes 1572896 | tf_op jit(solution)/shard_map/ppermute | solution.py:19
  216.9 2.1 copy.84
  219.0 2.4 reshape.635
  221.4 3.5 copy.85
  224.9 2.5 gather_fusion
  228.9 12.2 %scatter_fusion = f32[24,16384]{0,1:T(8,128)} fusion(f32[24,16384]{0,1:T(8,128)} %copy.95, s32[2048]{0:T(1024)S(1)} %bitcast.179, f32[2048,24]{1,0:T(8,128)S(1)} %copy.96), kind=kCustom, calls=%fused_computation.6 | custom fusion | bytes 598016 | tf_op jit(solution)/shard_map/scatter | solution.py:177
  241.1 5.1 %copy.97 = f32[24,16384]{1,0:T(8,128)S(1)} copy(f32[24,16384]{0,1:T(8,128)} %scatter_fusion) | data formatting | bytes 3145728 | tf_op jit(solution)/shard_map/scatter | solution.py:177
  246.5 1.3 collective-permute-start.2
  247.8 3.0 collective-permute-start.3
  250.9 0.8 collective-permute-done.3
  251.8 2.3 fusion.116
  254.1 2.3 copy.100
  256.4 7.6 %collective-permute-start.5 = (f32[6,4,130,1]{2,1,3,0:T(4,128)S(1)}, f32[6,4,130,1]{2,1,3,0:T(4,128)S(1)}, u32[]{:S(2)}, u32[]{:S(2)}) collective-permute-start(f32[6,4,130,1]{2,1,3,0:T(4,128)S(1)} %copy.100), channel_id=1, source_target_pairs={{0,1},{1,2},{2,3},{3,4},{4,5},{5,6},{6,7},{7,8},{8,9},{9,10},{10,1... | collective-permute-start | bytes 37448 | tf_op jit(solution)/shard_map/ppermute | solution.py:29
  264.1 2.3 copy.98
  266.4 4.8 %collective-permute-start.4 = (f32[6,4,130,1]{2,1,3,0:T(4,128)S(1)}, f32[6,4,130,1]{2,1,3,0:T(4,128)S(1)}, u32[]{:S(2)}, u32[]{:S(2)}) collective-permute-start(f32[6,4,130,1]{2,1,3,0:T(4,128)S(1)} %copy.98), channel_id=1, source_target_pairs={{1,0},{2,1},{3,2},{4,3},{5,4},{6,5},{7,6},{8,7},{9,8},{10,9},{11,1... | collective-permute-start | bytes 37448 | tf_op jit(solution)/shard_map/ppermute | solution.py:30
  271.2 6.6 %slice_multiply_fusion = f32[4,16384]{0,1:T(8,128)} fusion(f32[24,16384]{0,1:T(8,128)} %scatter_fusion), kind=kLoop, calls=%fused_computation.7 | loop fusion | flops 65536 | bytes 524288 | tf_op jit(solution)/shard_map/mul | solution.py:184
  277.8 5.2 %copy.102 = f32[1,4,128,128]{3,2,1,0:T(8,128)S(1)} copy(f32[1,4,128,128]{1,3,2,0:T(8,128)} %bitcast.153) | data formatting | bytes 524288 | tf_op jit(solution)/shard_map/mul | solution.py:184
  283.1 1.8 copy.101
  284.9 1.8 copy.99
  286.6 3.5 fusion.4
  290.3 1.3 collective-permute-start.6
  291.6 3.4 collective-permute-start.7
  295.9 1.4 fusion.118
  297.4 1.6 copy.103
  299.0 5.1 %collective-permute-start.8 = (f32[3,4,130,1]{2,1,3,0:T(4,128)S(1)}, f32[3,4,130,1]{2,1,3,0:T(4,128)S(1)}, u32[]{:S(2)}, u32[]{:S(2)}) collective-permute-start(f32[3,4,130,1]{2,1,3,0:T(4,128)S(1)} %copy.103), channel_id=1, source_target_pairs={{1,0},{2,1},{3,2},{4,3},{5,4},{6,5},{7,6},{8,7},{9,8},{10,9},{11,1... | collective-permute-start | bytes 18728 | tf_op jit(solution)/shard_map/ppermute | solution.py:30
  304.1 1.6 copy.105
  305.8 2.2 collective-permute-start.9
  308.0 1.3 copy.104
  309.3 4.5 %collective-permute-done.9 = f32[3,4,130,1]{2,1,3,0:T(4,128)S(1)} collective-permute-done((f32[3,4,130,1]{2,1,3,0:T(4,128)S(1)}, f32[3,4,130,1]{2,1,3,0:T(4,128)S(1)}, u32[]{:S(2)}, u32[]{:S(2)}) %collective-permute-start.9) | collective-permute-done | bytes 6272 | tf_op jit(solution)/shard_map/ppermute | solution.py:29
  313.8 1.2 copy.106
  315.0 1.4 broadcast_divide_fusion
  316.4 1.3 collective-permute-start.10
  317.7 3.9 collective-permute-start.11
  321.6 0.8 collective-permute-done.11
  322.6 2.5 collective-permute-start.12
  325.0 4.9 %collective-permute-start.13 = (f32[4,130,1]{2,1,0:T(8,128)S(1)}, f32[4,130,1]{2,1,0:T(8,128)S(1)}, u32[]{:S(2)}, u32[]{:S(2)}) collective-permute-start(f32[4,130,1]{2,1,0:T(8,128)S(1)} %get-tuple-element.24), channel_id=1, source_target_pairs={{0,1},{1,2},{2,3},{3,4},{4,5},{5,6},{6,7},{7,8},{8,9},{9,10},{10,1... | collective-permute-start | bytes 6248 | tf_op jit(solution)/shard_map/ppermute | solution.py:29
  329.9 2.8 collective-permute-done.12
  332.8 4.1 %collective-permute-done.13 = f32[4,130,1]{2,1,0:T(8,128)S(1)} collective-permute-done((f32[4,130,1]{2,1,0:T(8,128)S(1)}, f32[4,130,1]{2,1,0:T(8,128)S(1)}, u32[]{:S(2)}, u32[]{:S(2)}) %collective-permute-start.13) | collective-permute-done | bytes 2112 | tf_op jit(solution)/shard_map/ppermute | solution.py:29
  337.9 19.3 %all-to-all-start.2 = ((f32[256,4,1]{1,2,0:T(1,128)}), f32[256,4,1]{1,2,0:T(1,128)S(1)}, u32[]{:S(2)}, u32[]{:S(2)}) async-start(f32[256,4,1]{1,2,0:T(1,128)} %stack.44), calls=%async_computation.2 | async-start | bytes 262144 | tf_op jit(solution)/shard_map/all_to_all | solution.py:193
  357.3 19.2 %all-to-all-done.2 = f32[256,4,1]{1,2,0:T(1,128)S(1)} async-done(((f32[256,4,1]{1,2,0:T(1,128)}), f32[256,4,1]{1,2,0:T(1,128)S(1)}, u32[]{:S(2)}, u32[]{:S(2)}) %all-to-all-start.2) | async-done | bytes 4128 | tf_op jit(solution)/shard_map/all_to_all | solution.py:193
  379.0 1.3 collective-permute-start.14
  380.3 3.1 collective-permute-start.15
  384.3 3.7 collective-permute-start.16
  388.0 3.7 collective-permute-start.17
  391.7 0.8 fusion.128
  392.5 10.1 %collective-permute-done.16 = f32[4,130,1]{2,1,0:T(8,128)S(1)} collective-permute-done((f32[4,130,1]{2,1,0:T(8,128)S(1)}, f32[4,130,1]{2,1,0:T(8,128)S(1)}, u32[]{:S(2)}, u32[]{:S(2)}) %collective-permute-start.16) | collective-permute-done | bytes 2112 | tf_op jit(solution)/shard_map/ppermute | solution.py:30
  402.9 1.3 maximum_bitcast_fusion
  (99 shorter events, 14.7 us)
Async XLA Ops:
  4.5 5.7 %collective-permute-start = (s32[32,128]{1,0:T(8,128)S(1)}, s32[32,128]{1,0:T(8,128)}, u32[]{:S(2)}, u32[]{:S(2)}) collective-permute-start(s32[32,128]{1,0:T(8,128)S(1)} %reshape.634), channel_id=1, source_target_pairs={{0,256},{256,0},{1,257},{257,1},{2,258},{258,2},{3,259},{259,3},{4... | collective-permute-start | bytes 49160 | tf_op jit(solution)/shard_map/ppermute | solution.py:19
  10.2 31.2 %all-to-all-start = ((s32[32,1,128]{2,1,0:T(1,128)}), s32[32,1,128]{2,1,0:T(1,128)S(1)}, u32[]{:S(2)}, u32[]{:S(2)}) async-start(s32[32,1,128]{2,1,0:T(1,128)} %bitcast.6), calls=%async_computation | async-start | bytes 32768 | tf_op jit(solution)/shard_map/all_to_all | solution.py:147
  101.1 1.0 copy-start
  103.5 85.4 %copy-start.2 = (s32[1,1,2048]{2,1,0:T(1,128)S(1)}, s32[1,1,2048]{2,1,0:T(1,128)}, u32[]{:S(2)}) copy-start(s32[1,1,2048]{2,1,0:T(1,128)} %param.15) | copy-start | bytes 24580
  103.5 86.3 %copy-start.3 = (s32[1,1,2048]{2,1,0:T(1,128)S(1)}, s32[1,1,2048]{2,1,0:T(1,128)}, u32[]{:S(2)}) copy-start(s32[1,1,2048]{2,1,0:T(1,128)} %param.17) | copy-start | bytes 24580
  103.5 86.3 %copy-start.1 = (f32[1,1,2048]{2,1,0:T(1,128)S(1)}, f32[1,1,2048]{2,1,0:T(1,128)}, u32[]{:S(2)}) copy-start(f32[1,1,2048]{2,1,0:T(1,128)} %param.16) | copy-start | bytes 24580
  103.5 82.3 %all-to-all-start.1 = ((f32[4,24,32,128]{3,1,0,2:T(8,128)}), f32[4,24,32,128]{3,1,0,2:T(8,128)S(1)}, u32[]{:S(2)}, u32[]{:S(2)}) async-start(f32[4,24,32,128]{3,1,0,2:T(8,128)} %pad_maximum_fusion.9), calls=%async_computation.1 | async-start | bytes 3145728 | tf_op jit(solution)/shard_map/all_to_all | solution.py:157
  185.8 31.2 %collective-permute-start.1 = (f32[4,24,32,128]{3,1,0,2:T(8,128)S(1)}, f32[4,24,32,128]{3,1,0,2:T(8,128)S(1)}, u32[]{:S(2)}, u32[]{:S(2)}) collective-permute-start(f32[4,24,32,128]{3,1,0,2:T(8,128)S(1)} %all-to-all-done.1), channel_id=1, source_target_pairs={{0,256},{256,0},{1,257},{257,1},{2,258},{258,2},{3,259},{259,3},{4... | collective-permute-start | bytes 4718600 | tf_op jit(solution)/shard_map/ppermute | solution.py:19
  246.5 4.4 %collective-permute-start.2 = (f32[6,4,1,128]{3,2,1,0:T(1,128)S(1)}, f32[6,4,1,128]{3,2,1,0:T(1,128)S(1)}, u32[]{:S(2)}, u32[]{:S(2)}) collective-permute-start(f32[6,4,1,128]{3,2,1,0:T(1,128)S(1)} %get-tuple-element.12), channel_id=1, source_target_pairs={{32,0},{64,32},{96,64},{128,96},{160,128},{192,160},{224,192},{33,... | collective-permute-start | bytes 36872 | tf_op jit(solution)/shard_map/ppermute | solution.py:30
  247.8 3.9 collective-permute-start.3
  256.4 26.6 %collective-permute-start.5 = (f32[6,4,130,1]{2,1,3,0:T(4,128)S(1)}, f32[6,4,130,1]{2,1,3,0:T(4,128)S(1)}, u32[]{:S(2)}, u32[]{:S(2)}) collective-permute-start(f32[6,4,130,1]{2,1,3,0:T(4,128)S(1)} %copy.100), channel_id=1, source_target_pairs={{0,1},{1,2},{2,3},{3,4},{4,5},{5,6},{6,7},{7,8},{8,9},{9,10},{10,1... | collective-permute-start | bytes 37448 | tf_op jit(solution)/shard_map/ppermute | solution.py:29
  266.4 18.4 %collective-permute-start.4 = (f32[6,4,130,1]{2,1,3,0:T(4,128)S(1)}, f32[6,4,130,1]{2,1,3,0:T(4,128)S(1)}, u32[]{:S(2)}, u32[]{:S(2)}) collective-permute-start(f32[6,4,130,1]{2,1,3,0:T(4,128)S(1)} %copy.98), channel_id=1, source_target_pairs={{1,0},{2,1},{3,2},{4,3},{5,4},{6,5},{7,6},{8,7},{9,8},{10,9},{11,1... | collective-permute-start | bytes 37448 | tf_op jit(solution)/shard_map/ppermute | solution.py:30
  290.3 4.8 %collective-permute-start.6 = (f32[3,4,1,128]{3,2,1,0:T(1,128)S(1)}, f32[3,4,1,128]{3,2,1,0:T(1,128)S(1)}, u32[]{:S(2)}, u32[]{:S(2)}) collective-permute-start(f32[3,4,1,128]{3,2,1,0:T(1,128)S(1)} %get-tuple-element.10), channel_id=1, source_target_pairs={{32,0},{64,32},{96,64},{128,96},{160,128},{192,160},{224,192},{33,... | collective-permute-start | bytes 18440 | tf_op jit(solution)/shard_map/ppermute | solution.py:30
  291.6 4.3 %collective-permute-start.7 = (f32[3,4,1,128]{3,2,1,0:T(1,128)S(1)}, f32[3,4,1,128]{3,2,1,0:T(1,128)S(1)}, u32[]{:S(2)}, u32[]{:S(2)}) collective-permute-start(f32[3,4,1,128]{3,2,1,0:T(1,128)S(1)} %get-tuple-element.9), channel_id=1, source_target_pairs={{0,32},{32,64},{64,96},{96,128},{128,160},{160,192},{192,224},{1,3... | collective-permute-start | bytes 18440 | tf_op jit(solution)/shard_map/ppermute | solution.py:29
  299.0 9.0 %collective-permute-start.8 = (f32[3,4,130,1]{2,1,3,0:T(4,128)S(1)}, f32[3,4,130,1]{2,1,3,0:T(4,128)S(1)}, u32[]{:S(2)}, u32[]{:S(2)}) collective-permute-start(f32[3,4,130,1]{2,1,3,0:T(4,128)S(1)} %copy.103), channel_id=1, source_target_pairs={{1,0},{2,1},{3,2},{4,3},{5,4},{6,5},{7,6},{8,7},{9,8},{10,9},{11,1... | collective-permute-start | bytes 18728 | tf_op jit(solution)/shard_map/ppermute | solution.py:30
  305.8 8.0 %collective-permute-start.9 = (f32[3,4,130,1]{2,1,3,0:T(4,128)S(1)}, f32[3,4,130,1]{2,1,3,0:T(4,128)S(1)}, u32[]{:S(2)}, u32[]{:S(2)}) collective-permute-start(f32[3,4,130,1]{2,1,3,0:T(4,128)S(1)} %copy.105), channel_id=1, source_target_pairs={{0,1},{1,2},{2,3},{3,4},{4,5},{5,6},{6,7},{7,8},{8,9},{9,10},{10,1... | collective-permute-start | bytes 18728 | tf_op jit(solution)/shard_map/ppermute | solution.py:29
  316.4 5.2 %collective-permute-start.10 = (f32[4,1,128]{2,1,0:T(1,128)S(1)}, f32[4,1,128]{2,1,0:T(1,128)S(1)}, u32[]{:S(2)}, u32[]{:S(2)}) collective-permute-start(f32[4,1,128]{2,1,0:T(1,128)S(1)} %get-tuple-element.29), channel_id=1, source_target_pairs={{32,0},{64,32},{96,64},{128,96},{160,128},{192,160},{224,192},{33,... | collective-permute-start | bytes 6152 | tf_op jit(solution)/shard_map/ppermute | solution.py:30
  317.7 4.7 %collective-permute-start.11 = (f32[4,1,128]{2,1,0:T(1,128)S(1)}, f32[4,1,128]{2,1,0:T(1,128)S(1)}, u32[]{:S(2)}, u32[]{:S(2)}) collective-permute-start(f32[4,1,128]{2,1,0:T(1,128)S(1)} %get-tuple-element.28), channel_id=1, source_target_pairs={{0,32},{32,64},{64,96},{96,128},{128,160},{160,192},{192,224},{1,3... | collective-permute-start | bytes 6152 | tf_op jit(solution)/shard_map/ppermute | solution.py:29
  322.6 10.2 %collective-permute-start.12 = (f32[4,130,1]{2,1,0:T(8,128)S(1)}, f32[4,130,1]{2,1,0:T(8,128)S(1)}, u32[]{:S(2)}, u32[]{:S(2)}) collective-permute-start(f32[4,130,1]{2,1,0:T(8,128)S(1)} %get-tuple-element.23), channel_id=1, source_target_pairs={{1,0},{2,1},{3,2},{4,3},{5,4},{6,5},{7,6},{8,7},{9,8},{10,9},{11,1... | collective-permute-start | bytes 6248 | tf_op jit(solution)/shard_map/ppermute | solution.py:30
  325.0 11.8 %collective-permute-start.13 = (f32[4,130,1]{2,1,0:T(8,128)S(1)}, f32[4,130,1]{2,1,0:T(8,128)S(1)}, u32[]{:S(2)}, u32[]{:S(2)}) collective-permute-start(f32[4,130,1]{2,1,0:T(8,128)S(1)} %get-tuple-element.24), channel_id=1, source_target_pairs={{0,1},{1,2},{2,3},{3,4},{4,5},{5,6},{6,7},{7,8},{8,9},{9,10},{10,1... | collective-permute-start | bytes 6248 | tf_op jit(solution)/shard_map/ppermute | solution.py:29
  337.9 38.5 %all-to-all-start.2 = ((f32[256,4,1]{1,2,0:T(1,128)}), f32[256,4,1]{1,2,0:T(1,128)S(1)}, u32[]{:S(2)}, u32[]{:S(2)}) async-start(f32[256,4,1]{1,2,0:T(1,128)} %stack.44), calls=%async_computation.2 | async-start | bytes 262144 | tf_op jit(solution)/shard_map/all_to_all | solution.py:193
  379.0 4.5 %collective-permute-start.14 = (f32[4,1,128]{2,1,0:T(1,128)S(1)}, f32[4,1,128]{2,1,0:T(1,128)S(1)}, u32[]{:S(2)}, u32[]{:S(2)}) collective-permute-start(f32[4,1,128]{2,1,0:T(1,128)S(1)} %get-tuple-element.27), channel_id=1, source_target_pairs={{32,0},{64,32},{96,64},{128,96},{160,128},{192,160},{224,192},{33,... | collective-permute-start | bytes 6152 | tf_op jit(solution)/shard_map/ppermute | solution.py:30
  380.3 3.9 collective-permute-start.15
  384.3 18.3 %collective-permute-start.16 = (f32[4,130,1]{2,1,0:T(8,128)S(1)}, f32[4,130,1]{2,1,0:T(8,128)S(1)}, u32[]{:S(2)}, u32[]{:S(2)}) collective-permute-start(f32[4,130,1]{2,1,0:T(8,128)S(1)} %get-tuple-element.21), channel_id=1, source_target_pairs={{1,0},{2,1},{3,2},{4,3},{5,4},{6,5},{7,6},{8,7},{9,8},{10,9},{11,1... | collective-permute-start | bytes 6248 | tf_op jit(solution)/shard_map/ppermute | solution.py:30
  388.0 14.6 %collective-permute-start.17 = (f32[4,130,1]{2,1,0:T(8,128)S(1)}, f32[4,130,1]{2,1,0:T(8,128)S(1)}, u32[]{:S(2)}, u32[]{:S(2)}) collective-permute-start(f32[4,130,1]{2,1,0:T(8,128)S(1)} %get-tuple-element.22), channel_id=1, source_target_pairs={{0,1},{1,2},{2,3},{3,4},{4,5},{5,6},{6,7},{7,8},{8,9},{9,10},{10,1... | collective-permute-start | bytes 6248 | tf_op jit(solution)/shard_map/ppermute | solution.py:29
